TPU v7x, 32 devices: a whole 2x2x4 slice. The times are simulated.
32 devices in a mesh: grp: 2 (over y), frame: 4 (over x, core), coil: 4 (over z).
Axes of the slice: x: 2, y: 2, z: 4, core: 2. Of those that a mesh axis runs over, the one named last changes fastest.
Arguments:
- images: bfloat16 [8, 2, 384, 384], P(('grp', 'frame')), parts along dimension 0, may hold values from -6 to 6
- coil_maps: bfloat16 [8, 2, 384, 384], P(('grp', 'coil')), parts along dimension 0, may hold values from -3 to 3
- kspace_data: float32 [8, 4, 2, 6, 128], P(('grp', 'frame'), 'coil'), parts along dimension 0, may hold values from -6 to 6
- spoke_angle: int32 [8, 6], P(('grp', 'frame')), parts along dimension 0, may hold values from 0 to 15
- band_row: int32 [8, 6], P(('grp', 'frame')), parts along dimension 0, may hold values from 0 to 256
- band_col: int32 [8, 6], P(('grp', 'frame')), parts along dimension 0, may hold values from 0 to 256
- kernel_rows: bfloat16 [16, 128, 128], replicated, may hold values from -0.5 to 0.5
- kernel_cols: bfloat16 [16, 128, 128], replicated, may hold values from -0.5 to 0.5
Outputs:
- updated: float32 [8, 2, 384, 384], P(('grp', 'frame')), parts along dimension 0
There are 2 independent parts, one for each index of `grp`. A program takes and returns all parts, laid end to end along the dimension named above; an argument that names none is the same for every part. Nothing has to cross between parts.
All inputs are finite; a program needn't handle non-finite values.
Results may differ from a plain program's by a relative error of at most 0.0014.
Values may be sent and summed in bfloat16 or wider, within the bound.
No kernel may reach another device: no remote copies, remote signals or barrier semaphores. Data moves between devices by JAX's collectives and lax.ppermute only.
A program may use at most 64 MiB of HBM per device.

v0:
```python
import math

import jax
import jax.numpy as jnp
from jax import lax
from jax.sharding import PartitionSpec as P

SMOOTHING = 0.05
STEP_SIZE = 1.0
TV_WEIGHT = 0.2


def padded(cells, sides, width):
    for axis, dim in sides:
        count = lax.axis_size(axis)
        ends = count - 1
        head = lax.slice_in_dim(cells, 0, width, axis=dim)
        tail = lax.slice_in_dim(cells, cells.shape[dim] - width, cells.shape[dim], axis=dim)
        cells = jnp.concatenate(
            [
                lax.ppermute(tail, axis, [(i, (i + 1) % count) for i in range(ends)]),
                cells,
                lax.ppermute(head, axis, [((i + 1) % count, i) for i in range(ends)]),
            ],
            axis=dim,
        )
    return cells


def transform_table(extent):
    indices = jnp.arange(extent, dtype=jnp.int32)
    phases = indices[:, None] * indices[None, :] % extent
    angle_values = 2.0 * math.pi / extent * phases.astype(jnp.float32)
    scaling = 1.0 / math.sqrt(extent)
    return jnp.stack([jnp.cos(angle_values) * scaling, jnp.sin(angle_values) * scaling]).astype(
        jnp.bfloat16
    )


def combine_parts(products, direction):
    real_part = products[0, 0] + direction * products[1, 1]
    imaginary = products[0, 1] - direction * products[1, 0]
    return jnp.stack([real_part, imaginary])


def left_apply(transform, planes, direction):
    products = jnp.einsum("aij,bjk->abik", transform, planes, preferred_element_type=jnp.float32)
    return combine_parts(products, direction)


def right_apply(transform, planes, direction):
    products = jnp.einsum("bij,ajk->abik", planes, transform, preferred_element_type=jnp.float32)
    return combine_parts(products, direction)


def selector(first_index, extent, patch_side, kind):
    positions = jnp.arange(extent, dtype=jnp.int32)
    offsets = jnp.arange(patch_side, dtype=jnp.int32)
    wanted = first_index[:, None, None] + offsets[None, None, :]
    return (positions[None, :, None] == wanted).astype(kind)


def cut_windows(kspace, row_first, col_first, patch_side):
    extent = kspace.shape[-1]
    row_select = selector(row_first, extent, patch_side, jnp.bfloat16)
    col_select = selector(col_first, extent, patch_side, jnp.bfloat16)
    picked_rows = jnp.einsum(
        "tir,bik->tbrk", row_select, kspace, preferred_element_type=jnp.float32
    ).astype(jnp.bfloat16)
    return jnp.einsum(
        "tbrk,tkq->tbrq", picked_rows, col_select, preferred_element_type=jnp.float32
    ).astype(jnp.bfloat16)


def add_windows(windows, row_first, col_first, extent):
    patch_side = windows.shape[-1]
    row_select = selector(row_first, extent, patch_side, jnp.float32)
    col_select = selector(col_first, extent, patch_side, jnp.float32)
    placed = jnp.einsum("tbrq,tkq->tbrk", windows, col_select, precision=lax.Precision.HIGHEST)
    return jnp.einsum("tir,tbrk->bik", row_select, placed, precision=lax.Precision.HIGHEST)


def coil_gradient(
    transform,
    frame_image,
    coil_map,
    measured,
    angle_ids,
    row_first,
    col_first,
    kernel_rows,
    kernel_cols,
):
    extent = frame_image.shape[-1]
    patch_side = kernel_cols.shape[-1]
    map_planes = coil_map.astype(jnp.float32)
    image_planes = frame_image.astype(jnp.float32)
    coil_image = jnp.stack(
        [
            map_planes[0] * image_planes[0] - map_planes[1] * image_planes[1],
            map_planes[0] * image_planes[1] + map_planes[1] * image_planes[0],
        ]
    ).astype(jnp.bfloat16)
    half_done = left_apply(transform, coil_image, 1.0).astype(jnp.bfloat16)
    kspace = right_apply(transform, half_done, 1.0).astype(jnp.bfloat16)
    patches = cut_windows(kspace, row_first, col_first, patch_side)
    row_weights = kernel_rows[angle_ids]
    col_weights = kernel_cols[angle_ids]
    contracted = jnp.einsum(
        "tprq,tjq->ptrj", patches, col_weights, preferred_element_type=jnp.float32
    )
    predicted = jnp.sum(contracted * row_weights[None], axis=2)
    residual = predicted - measured
    spread = (row_weights[None] * residual[:, :, None, :]).astype(jnp.bfloat16)
    spread_back = jnp.einsum(
        "ptrj,tjq->tprq", spread, col_weights, preferred_element_type=jnp.float32
    )
    gridded = add_windows(spread_back, row_first, col_first, extent)
    gridded = gridded.astype(jnp.bfloat16)
    half_back = left_apply(transform, gridded, -1.0).astype(jnp.bfloat16)
    coil_back = right_apply(transform, half_back, -1.0)
    return jnp.stack(
        [
            map_planes[0] * coil_back[0] + map_planes[1] * coil_back[1],
            map_planes[0] * coil_back[1] - map_planes[1] * coil_back[0],
        ]
    )


def apply_update(own_rows, extended, data_grad, first_frame, frame_total):
    widened = extended.astype(jnp.float32)
    change = widened[1:] - widened[:-1]
    position = first_frame - 1 + jnp.arange(change.shape[0], dtype=jnp.int32)
    inside = ((position >= 0) & (position <= frame_total - 2)).astype(jnp.float32)
    normed = inside[:, None, None, None] * (
        change / jnp.sqrt(jnp.sum(change * change, axis=1, keepdims=True) + SMOOTHING)
    )
    tv_grad = normed[:-1] - normed[1:]
    return own_rows.astype(jnp.float32) - STEP_SIZE * (data_grad + TV_WEIGHT * tv_grad)


def local(
    images, coil_maps, kspace_data, spoke_angle, band_row, band_col, kernel_rows, kernel_cols
):
    frame_count = images.shape[0]
    transform = transform_table(images.shape[-1])
    running = coil_gradient(
        transform,
        images[0],
        coil_maps[0],
        kspace_data[0, 0],
        spoke_angle[0],
        band_row[0],
        band_col[0],
        kernel_rows,
        kernel_cols,
    )
    gradients = [running]
    data_terms = jnp.stack(gradients)
    first_frame = lax.axis_index("frame") * frame_count
    frame_total = lax.axis_size("frame") * frame_count
    extended = padded(images, (("frame", 0),), 1)
    data_grad = lax.psum(data_terms.astype(jnp.bfloat16), "coil").astype(jnp.float32)
    return apply_update(images, extended, data_grad, first_frame, frame_total)


def solution(mesh):
    in_specs = (
        P(("grp", "frame"), None, None, None),
        P(("grp", "coil"), None, None, None),
        P(("grp", "frame"), "coil", None, None, None),
        P(("grp", "frame"), None),
        P(("grp", "frame"), None),
        P(("grp", "frame"), None),
        P(),
        P(),
    )
    out_specs = P(("grp", "frame"), None, None, None)
    return jax.shard_map(local, mesh=mesh, in_specs=in_specs, out_specs=out_specs, check_vma=False)
```

profile of v0, /device:TPU:0, one launch (start us, length us, event | category | flops | bytes accessed | tf_op | source)
XLA Modules:
  0.0 91.9 jit_solution(15855914148542029132)
XLA Ops:
  6.5 1.4 %copy.23 = bf16[1,2,384,384]{2,3,1,0:T(8,128)(2,1)S(1)} copy(bf16[1,2,384,384]{3,2,1,0:T(8,128)(2,1)} %param.8) | data formatting | bytes 1179648 | tf_op args[0]
  8.0 1.4 %collective-permute-start.1 = (bf16[1,2,384,384]{2,3,1,0:T(8,128)(2,1)S(1)}, bf16[1,2,384,384]{2,3,1,0:T(8,128)(2,1)}, u32[]{:S(2)}, u32[]{:S(2)}) collective-permute-start(bf16[1,2,384,384]{2,3,1,0:T(8,128)(2,1)S(1)} %copy.23), channel_id=1, source_target_pairs={{4,0},{8,4},{12,8},{5,1},{9,5},{13,9},{6,2},{10,6},{14,10},{7,3},{... | collective-permute-start | bytes 1769480 | tf_op jit(solution)/shard_map/ppermute | solution.py:23
  9.4 3.9 %collective-permute-start = (bf16[1,2,384,384]{2,3,1,0:T(8,128)(2,1)S(1)}, bf16[1,2,384,384]{2,3,1,0:T(8,128)(2,1)}, u32[]{:S(2)}, u32[]{:S(2)}) collective-permute-start(bf16[1,2,384,384]{2,3,1,0:T(8,128)(2,1)S(1)} %copy.23), channel_id=1, source_target_pairs={{0,4},{4,8},{8,12},{1,5},{5,9},{9,13},{2,6},{6,10},{10,14},{3,7},{... | collective-permute-start | bytes 1769480 | tf_op jit(solution)/shard_map/ppermute | solution.py:21
  13.3 1.1 %convert_element_type.83 = f32[1,2,384,384]{2,3,1,0:T(8,128)} convert(bf16[1,2,384,384]{2,3,1,0:T(8,128)(2,1)S(1)} %copy.23) | non-fusion elementwise | flops 294912 | bytes 1769472 | tf_op jit(solution)/shard_map/convert_element_type | solution.py:139
  14.4 2.6 %multiply_convert_fusion.1 = (bf16[1,384,384]{2,1,0:T(8,128)(2,1)S(1)}, bf16[1,384,384]{2,1,0:T(8,128)(2,1)S(1)}) fusion(), kind=kLoop, calls=%fused_computation.82 | loop fusion | flops 1916928 | bytes 589824 | tf_op jit(solution)/shard_map/convert.19
  17.0 0.3 copy.24
  17.4 1.2 %copy-done.1 = f32[1,2,384,384]{2,3,1,0:T(8,128)S(1)} copy-done((f32[1,2,384,384]{2,3,1,0:T(8,128)S(1)}, f32[1,2,384,384]{2,3,1,0:T(8,128)}, u32[]{:S(2)}) %copy-start.1) | copy-done | bytes 1179672
  18.6 0.2 fusion.53
  18.7 0.8 convolution_bitcast_fusion.3
  19.7 0.5 copy-done.6
  20.2 0.8 convolution_bitcast_fusion.2
  21.2 0.5 copy-done.4
  21.8 0.8 fusion.11
  22.6 2.0 %copy.70 = bf16[2,384,6,128]{3,2,1,0:T(8,128)(2,1)} copy(bf16[2,384,6,128]{3,1,2,0:T(8,128)(2,1)S(1)} %fusion.11) | data formatting | bytes 2359296 | tf_op jit(solution)/shard_map/tir,bik->tbrk/dot_general | solution.py:67
  24.7 0.6 gather_fusion.1
  25.3 1.6 %gather_fusion = bf16[6,128,128]{2,1,0:T(8,128)(2,1)S(1)} fusion(bf16[16,128,128]{2,1,0:T(8,128)(2,1)} %param.14, s32[1024]{0:T(1024)S(1)} %pad_clamp_fusion), kind=kCustom, calls=%fused_computation | custom fusion | bytes 393240 | tf_op jit(solution)/shard_map/gather | solution.py:107
  26.9 2.0 %convolution_convert_fusion = bf16[6,2,128,128]{3,2,1,0:T(8,128)(2,1)S(1)} fusion(bf16[6,2,128,384]{2,0,3,1:T(8,128)(2,1)} %bitcast.119, s32[6,128]{1,0:T(8,128)S(1)} %iota_add_fusion), kind=kOutput, calls=%fused_computation.17 | convolution fusion | flops 151486464 | bytes 1575936 | tf_op jit(solution)/shard_map/tbrk,tkq->tbrq/dot_general | solution.py:70
  29.0 0.3 fusion.4
  29.3 0.3 fusion.50
  29.6 1.1 %fusion.15 = f32[6,2,128,384]{3,2,1,0:T(8,128)S(1)} fusion(f32[6,2,128,128]{3,2,1,0:T(8,128)S(1)} %fusion.50, s32[6,128]{1,0:T(8,128)S(1)} %iota_add_fusion), kind=kOutput, calls=%fused_computation.31 | convolution fusion | flops 906264576 | bytes 3148800 | tf_op jit(solution)/shard_map/tbrq,tkq->tbrk/dot_general | solution.py:79
  30.7 3.9 %fusion.3 = bf16[2,384,384,1]{1,2,0,3:T(8,128)(2,1)S(1)} fusion(f32[6,2,128,384]{3,2,1,0:T(8,128)S(1)} %fusion.15, s32[6,128]{1,0:T(8,128)S(1)} %iota_add_fusion.1), kind=kOutput, calls=%fused_computation.16 | convolution fusion | flops 2718498816 | bytes 2952192 | tf_op jit(solution)/shard_map/tir,tbrk->bik/dot_general | solution.py:80
  34.6 0.8 convolution_bitcast_fusion.1
  35.6 0.8 convolution_bitcast_fusion
  36.4 0.3 add_convert_fusion
  36.6 0.9 pad_maximum_fusion.1
  37.6 1.5 %maximum_convert_fusion = f32[3,2,384,384]{2,3,1,0:T(8,128)S(1)} fusion(bf16[1,2,384,384]{2,3,1,0:T(8,128)(2,1)} %collective-permute-done.1, bf16[1,2,384,384]{2,3,1,0:T(8,128)(2,1)S(1)} %copy.23, bf16[1,2,384,384]{2,3,1,0:T(8,128)(2,1)} %collective-permute-done), kind=kLoop, calls=%fused_computation.6 | loop fusion | flops 2654208 | bytes 5308416 | tf_op jit(solution)/shard_map/convert_element_type | solution.py:131
  39.1 0.3 multiply_reduce_fusion
  39.4 0.3 add_sqrt_fusion
  39.7 0.3 divide_multiply_fusion
  40.0 40.0 %all-reduce.2.cloned.1.call-done = bf16[1,2,384,384]{2,3,1,0:T(8,128)(2,1)} async-done(((bf16[1,2,384,384]{2,3,1,0:T(8,128)(2,1)}), bf16[1,2,384,384]{2,3,1,0:T(8,128)(2,1)}) %all-reduce.2.cloned.1.call-update) | async-done | bytes 589840 | tf_op jit(solution)/shard_map/psum | solution.py:163
  80.0 2.3 %fusion.7 = f32[1,2,384,384]{2,3,1,0:T(8,128)} fusion(f32[2,2,384,384]{2,3,1,0:T(8,128)S(1)} %divide_multiply_fusion, bf16[1,2,384,384]{2,3,1,0:T(8,128)(2,1)} %all-reduce.2.cloned.1.call-done, bf16[1,2,384,384]{2,3,1,0:T(8,128)(2,1)S(1)} %copy.23), kind=kLoop, calls=%fused_computation.22 | loop fusion | flops 1769472 | bytes 4718592 | tf_op jit(solution)/shard_map/sub | solution.py:139
  82.4 2.7 %copy.36 = f32[1,2,384,384]{3,2,1,0:T(8,128)} copy(f32[1,2,384,384]{2,3,1,0:T(8,128)} %fusion.7) | data formatting | bytes 2359296 | tf_op jit(solution)/shard_map/sub | solution.py:139
  (27 shorter events, 0.7 us)
Async XLA Ops:
  6.5 18.1 %copy-start = (bf16[16,128,128]{2,1,0:T(8,128)(2,1)S(1)}, bf16[16,128,128]{2,1,0:T(8,128)(2,1)}, u32[]{:S(2)}) copy-start(bf16[16,128,128]{2,1,0:T(8,128)(2,1)} %param.15) | copy-start | bytes 1572868
  6.5 73.5 %all-reduce.2.cloned.1.call-start = ((), (), s32[]{:S(2)}) async-start(), calls=%async_computation | async-start | bytes 1179648 | tf_op jit(solution)/shard_map/psum | solution.py:163
  8.0 9.0 %copy-start.2 = (bf16[1,2,384,384]{3,2,1,0:T(8,128)(2,1)S(1)}, bf16[1,2,384,384]{3,2,1,0:T(8,128)(2,1)}, u32[]{:S(2)}) copy-start(bf16[1,2,384,384]{3,2,1,0:T(8,128)(2,1)} %param.9) | copy-start | bytes 1769476
  8.0 29.6 %collective-permute-start.1 = (bf16[1,2,384,384]{2,3,1,0:T(8,128)(2,1)S(1)}, bf16[1,2,384,384]{2,3,1,0:T(8,128)(2,1)}, u32[]{:S(2)}, u32[]{:S(2)}) collective-permute-start(bf16[1,2,384,384]{2,3,1,0:T(8,128)(2,1)S(1)} %copy.23), channel_id=1, source_target_pairs={{4,0},{8,4},{12,8},{5,1},{9,5},{13,9},{6,2},{10,6},{14,10},{7,3},{... | collective-permute-start | bytes 1769480 | tf_op jit(solution)/shard_map/ppermute | solution.py:23
  9.4 28.2 %collective-permute-start = (bf16[1,2,384,384]{2,3,1,0:T(8,128)(2,1)S(1)}, bf16[1,2,384,384]{2,3,1,0:T(8,128)(2,1)}, u32[]{:S(2)}, u32[]{:S(2)}) collective-permute-start(bf16[1,2,384,384]{2,3,1,0:T(8,128)(2,1)S(1)} %copy.23), channel_id=1, source_target_pairs={{0,4},{4,8},{8,12},{1,5},{5,9},{9,13},{2,6},{6,10},{10,14},{3,7},{... | collective-permute-start | bytes 1769480 | tf_op jit(solution)/shard_map/ppermute | solution.py:21
  17.3 1.3 %copy-start.1 = (f32[1,2,384,384]{2,3,1,0:T(8,128)S(1)}, f32[1,2,384,384]{2,3,1,0:T(8,128)}, u32[]{:S(2)}) copy-start(f32[1,2,384,384]{2,3,1,0:T(8,128)} %convert_element_type.83) | copy-start | bytes 3538948
  19.5 0.7 copy-start.6
  21.0 0.7 copy-start.4
  22.6 2.0 %copy-start.5 = (s32[1,6]{1,0:T(1,128)S(1)}, s32[1,6]{1,0:T(1,128)}, u32[]{:S(2)}) copy-start(s32[1,6]{1,0:T(1,128)} %param.13) | copy-start | bytes 76
  26.9 2.4 %copy-start.3 = (f32[1,1,2,6,128]{4,2,3,1,0:T(2,128)S(1)}, f32[1,1,2,6,128]{4,2,3,1,0:T(2,128)}, u32[]{:S(2)}) copy-start(f32[1,1,2,6,128]{4,2,3,1,0:T(2,128)} %param.10) | copy-start | bytes 18436
Sparse Core Ops, SparseCore 0:
  37.7 42.3 all-reduce.1
where the time goes:
time: 92.3 us; the launch traced here: 91.9 us
  waiting for transfers between devices  40 us (43%)
  between operations  13.7 us (15%)
  matrix products  11.7 us (13%)
  local copies, waits for them, and re-layouts  10.8 us (12%)
  other arithmetic  10.4 us (11%)
  starting transfers between devices  5.29 us (6%)
    psum x1, waiting for transfers between devices, local(): lax.psum(data_terms.astype(jnp.bfloat16), 'coil').astype(jnp.float32)  40 us
    unnamed x16, local copies, waits for them, and re-layouts  3.99 us
    dot_general x1, matrix products, add_windows(): jnp.einsum('tir,tbrk->bik', row_select, placed, precision=lax.Precision.H...  3.92 us
    ppermute x1, starting transfers between devices, padded(): lax.ppermute(tail, axis, [(i, (i + 1) % count) for i in range(ends)])  3.86 us
    another operation x2, other arithmetic  2.84 us
    sub x1, local copies, waits for them, and re-layouts, apply_update(): own_rows.astype(jnp.float32) - STEP_SIZE * (data_grad + TV_WEIGHT * tv_grad)  2.65 us
    sub x1, other arithmetic, apply_update(): own_rows.astype(jnp.float32) - STEP_SIZE * (data_grad + TV_WEIGHT * tv_grad)  2.33 us
    dot_general x1, matrix products, cut_windows(): jnp.einsum('tbrk,tkq->tbrq', picked_rows, col_select, preferred_element_t...  2.05 us
  transfers between devices with their start and end apart: 3, of which 1 were waited for; matrix products, arithmetic and copies ran while one was open for 26% of the time, Pallas kernels for 0%

commit v1 on v0

v1 whole, which is shorter than its diff:
```python
import math

import jax
import jax.numpy as jnp
from jax import lax
from jax.sharding import PartitionSpec as P

SMOOTHING = 0.05
STEP_SIZE = 1.0
TV_WEIGHT = 0.2


def padded(cells, sides, width):
    for axis, dim in sides:
        count = lax.axis_size(axis)
        ends = count - 1
        head = lax.slice_in_dim(cells, 0, width, axis=dim)
        tail = lax.slice_in_dim(cells, cells.shape[dim] - width, cells.shape[dim], axis=dim)
        cells = jnp.concatenate(
            [
                lax.ppermute(tail, axis, [(i, (i + 1) % count) for i in range(ends)]),
                cells,
                lax.ppermute(head, axis, [((i + 1) % count, i) for i in range(ends)]),
            ],
            axis=dim,
        )
    return cells


def transform_table(extent):
    indices = jnp.arange(extent, dtype=jnp.int32)
    phases = indices[:, None] * indices[None, :] % extent
    angle_values = 2.0 * math.pi / extent * phases.astype(jnp.float32)
    scaling = 1.0 / math.sqrt(extent)
    return jnp.stack([jnp.cos(angle_values) * scaling, jnp.sin(angle_values) * scaling]).astype(
        jnp.bfloat16
    )


def combine_parts(products, direction):
    real_part = products[0, 0] + direction * products[1, 1]
    imaginary = products[0, 1] - direction * products[1, 0]
    return jnp.stack([real_part, imaginary])


def apply_update(own_rows, extended, data_grad, first_frame, frame_total):
    widened = extended.astype(jnp.float32)
    change = widened[1:] - widened[:-1]
    position = first_frame - 1 + jnp.arange(change.shape[0], dtype=jnp.int32)
    inside = ((position >= 0) & (position <= frame_total - 2)).astype(jnp.float32)
    normed = inside[:, None, None, None] * (
        change / jnp.sqrt(jnp.sum(change * change, axis=1, keepdims=True) + SMOOTHING)
    )
    tv_grad = normed[:-1] - normed[1:]
    return own_rows.astype(jnp.float32) - STEP_SIZE * (data_grad + TV_WEIGHT * tv_grad)


def exchange_rows(coil_map, rows, coil_count, coil_index):
    received = [None] * coil_count
    received[0] = lax.dynamic_slice_in_dim(coil_map, coil_index * rows, rows, axis=1)
    for shift in range(1, coil_count):
        target = (coil_index + shift) % coil_count
        block = lax.dynamic_slice_in_dim(coil_map, target * rows, rows, axis=1)
        received[shift] = lax.ppermute(
            block, "coil", [(i, (i + shift) % coil_count) for i in range(coil_count)]
        )
    return jnp.stack(received)


def forward_residual(transform, frame_image, coil_map, measured, row_first, col_first, row_w, col_w):
    patch_side = col_w.shape[-1]
    map_planes = coil_map.astype(jnp.float32)
    image_planes = frame_image.astype(jnp.float32)
    coil_image = jnp.stack(
        [
            map_planes[0] * image_planes[0] - map_planes[1] * image_planes[1],
            map_planes[0] * image_planes[1] + map_planes[1] * image_planes[0],
        ]
    ).astype(jnp.bfloat16)
    products = jnp.einsum("aij,bjk->abik", transform, coil_image, preferred_element_type=jnp.float32)
    half_done = combine_parts(products, 1.0).astype(jnp.bfloat16)
    products = jnp.einsum("bij,ajk->abik", half_done, transform, preferred_element_type=jnp.float32)
    kspace = combine_parts(products, 1.0).astype(jnp.bfloat16)
    tiles = row_first.shape[0]
    patches = jnp.stack(
        [
            lax.dynamic_slice(kspace, (0, row_first[g], col_first[g]), (2, patch_side, patch_side))
            for g in range(tiles)
        ],
        axis=1,
    )
    contracted = jnp.einsum("pgrq,gjq->pgrj", patches, col_w, preferred_element_type=jnp.float32)
    predicted = jnp.sum(contracted * row_w.astype(jnp.float32)[None], axis=2)
    return predicted - measured


def backward_rows(transform, residuals, map_rows, row_first, col_first, row_w, col_w, coil_index):
    coil_count, _, rows, extent = map_rows.shape
    patch_side = col_w.shape[-1]
    spread = (row_w.astype(jnp.float32)[None, None] * residuals[:, :, :, None, :]).astype(jnp.bfloat16)
    spread_back = jnp.einsum("cpgrj,gjq->cpgrq", spread, col_w, preferred_element_type=jnp.float32)
    grid = jnp.zeros((coil_count, 2, extent, extent), jnp.float32)
    for g in range(row_first.shape[0]):
        start = (0, 0, row_first[g], col_first[g])
        window = lax.dynamic_slice(grid, start, (coil_count, 2, patch_side, patch_side))
        grid = lax.dynamic_update_slice(grid, window + spread_back[:, :, g], start)
    grid = grid.astype(jnp.bfloat16)
    row_table = lax.dynamic_slice_in_dim(transform, coil_index * rows, rows, axis=1)
    products = jnp.einsum("aij,cbjk->abcik", row_table, grid, preferred_element_type=jnp.float32)
    half_back = combine_parts(products, -1.0).astype(jnp.bfloat16)
    products = jnp.einsum("bcij,ajk->abcik", half_back, transform, preferred_element_type=jnp.float32)
    coil_back = combine_parts(products, -1.0)
    maps = map_rows.astype(jnp.float32)
    real_part = jnp.sum(maps[:, 0] * coil_back[0] + maps[:, 1] * coil_back[1], axis=0)
    imaginary = jnp.sum(maps[:, 0] * coil_back[1] - maps[:, 1] * coil_back[0], axis=0)
    return jnp.stack([real_part, imaginary])


def local(
    images, coil_maps, kspace_data, spoke_angle, band_row, band_col, kernel_rows, kernel_cols
):
    frame_count = images.shape[0]
    extent = images.shape[-1]
    coil_count = lax.axis_size("coil")
    coil_index = lax.axis_index("coil")
    rows = extent // coil_count
    transform = transform_table(extent)
    map_rows = exchange_rows(coil_maps[0], rows, coil_count, coil_index)
    first_frame = lax.axis_index("frame") * frame_count
    frame_total = lax.axis_size("frame") * frame_count
    extended = padded(images, (("frame", 0),), 1)
    row_w = kernel_rows[spoke_angle[0]]
    col_w = kernel_cols[spoke_angle[0]]
    residual = forward_residual(
        transform, images[0], coil_maps[0], kspace_data[0, 0], band_row[0], band_col[0], row_w, col_w
    )
    residuals = lax.all_gather(residual, "coil")
    sources = (coil_index - jnp.arange(coil_count, dtype=jnp.int32)) % coil_count
    residuals = jnp.take(residuals, sources, axis=0)
    grad_rows = backward_rows(
        transform, residuals, map_rows, band_row[0], band_col[0], row_w, col_w, coil_index
    )
    data_grad = lax.all_gather(grad_rows.astype(jnp.bfloat16), "coil", axis=1, tiled=True)
    data_grad = data_grad.astype(jnp.float32)[None]
    return apply_update(images, extended, data_grad, first_frame, frame_total)


def solution(mesh):
    in_specs = (
        P(("grp", "frame"), None, None, None),
        P(("grp", "coil"), None, None, None),
        P(("grp", "frame"), "coil", None, None, None),
        P(("grp", "frame"), None),
        P(("grp", "frame"), None),
        P(("grp", "frame"), None),
        P(),
        P(),
    )
    out_specs = P(("grp", "frame"), None, None, None)
    return jax.shard_map(local, mesh=mesh, in_specs=in_specs, out_specs=out_specs, check_vma=False)
```

time: 92.3 us -> 150 us (1.63); the launches traced: 91.9 us -> 148 us
  local copies, waits for them, and re-layouts: 10.8 us -> 62.5 us
  waiting for transfers between devices: 40 us -> 0.01 us
  blocking collectives: 0 us -> 28.7 us
  between operations: 13.7 us -> 22.9 us
  other arithmetic: 10.4 us -> 16.1 us
  starting transfers between devices: 5.29 us -> 10.9 us
  matrix products: 11.7 us -> 6.66 us
    dynamic_update_slice x0 -> x6, local copies, waits for them, and re-layouts: none -> 45.8 us  [backward_rows(): grid = lax.dynamic_update_slice(grid, window + spread_back[:, :, g], start)]
    psum x1 -> x0, waiting for transfers between devices: 40 us -> none  [local(): lax.psum(data_terms.astype(jnp.bfloat16), 'coil').astype(jnp.float32)]
    all_gather x0 -> x2, blocking collectives: none -> 28.7 us  [the longest x1 15.4 us: local(): lax.all_gather(grad_rows.astype(jnp.bfloat16), 'coil', axis=1, tiled=True)]
    add x2 -> x5, other arithmetic: 0.14 us -> 8.18 us  [backward_rows(): grid = lax.dynamic_update_slice(grid, window + spread_back[:, :, g], start)]
    ppermute x0 -> x3, starting transfers between devices: none -> 6.33 us  [exchange_rows(): lax.ppermute(block, 'coil', [(i, (i + shift) % coil_count) for i in range...]
    dot_general x10 -> x6, matrix products: 11.7 us -> 6.66 us  [the longest x1 3.3 us: backward_rows(): jnp.einsum('aij,cbjk->abcik', row_table, grid, preferred_element_type=jnp...]
    dynamic_slice x0 -> x8, local copies, waits for them, and re-layouts: none -> 3.51 us  [the longest x1 1.84 us: exchange_rows(): block = lax.dynamic_slice_in_dim(coil_map, target * rows, rows, axis=1)]
    broadcast_in_dim x0 -> x1, local copies, waits for them, and re-layouts: none -> 2.51 us  [backward_rows(): grid = jnp.zeros((coil_count, 2, extent, extent), jnp.float32)]
  transfers between devices with their start and end apart: 3 -> 5, of which waited for: 1 -> 0; matrix products, arithmetic and copies ran while one was open for 26% -> 53% of each run, Pallas kernels for 0% -> 0%
where the time goes in v1:
time: 150 us; the launch traced here: 148 us
  local copies, waits for them, and re-layouts  62.5 us (42%)
  blocking collectives  28.7 us (19%)
  between operations  22.9 us (15%)
  other arithmetic  16.1 us (11%)
  starting transfers between devices  10.9 us (7%)
  matrix products  6.66 us (4%)
    dynamic_update_slice x6, local copies, waits for them, and re-layouts, backward_rows(): grid = lax.dynamic_update_slice(grid, window + spread_back[:, :, g], start)  45.8 us
    all_gather x1, blocking collectives, local(): lax.all_gather(grad_rows.astype(jnp.bfloat16), 'coil', axis=1, tiled=True)  15.4 us
    all_gather x1, blocking collectives, local(): residuals = lax.all_gather(residual, 'coil')  13.3 us
    add x5, other arithmetic, backward_rows(): grid = lax.dynamic_update_slice(grid, window + spread_back[:, :, g], start)  8.18 us
    ppermute x3, starting transfers between devices, exchange_rows(): lax.ppermute(block, 'coil', [(i, (i + shift) % coil_count) for i in range...  6.33 us
    unnamed x21, local copies, waits for them, and re-layouts  4.01 us
    dot_general x1, matrix products, backward_rows(): jnp.einsum('aij,cbjk->abcik', row_table, grid, preferred_element_type=jnp...  3.3 us
    ppermute x1, starting transfers between devices, padded(): lax.ppermute(tail, axis, [(i, (i + 1) % count) for i in range(ends)])  3.28 us
  transfers between devices with their start and end apart: 5, of which 0 were waited for; matrix products, arithmetic and copies ran while one was open for 53% of the time, Pallas kernels for 0%

profile of v1, /device:TPU:0, one launch (start us, length us, event | category | flops | bytes accessed | tf_op | source)
XLA Modules:
  0.0 147.7 jit_solution(1502944840575813441)
XLA Ops:
  0.0 1.5 copy.49
  1.5 3.3 %collective-permute-start.3 = (bf16[1,2,384,384]{2,3,1,0:T(8,128)(2,1)S(1)}, bf16[1,2,384,384]{2,3,1,0:T(8,128)(2,1)}, u32[]{:S(2)}, u32[]{:S(2)}) collective-permute-start(bf16[1,2,384,384]{2,3,1,0:T(8,128)(2,1)S(1)} %copy.49), channel_id=1, source_target_pairs={{0,4},{4,8},{8,12},{1,5},{5,9},{9,13},{2,6},{6,10},{10,14},{3,7},{... | collective-permute-start | bytes 1769480 | tf_op jit(solution)/shard_map/ppermute | solution.py:21
  4.7 1.3 collective-permute-start.4
  6.1 1.8 %dynamic-slice_bitcast_fusion.2 = (bf16[2,96,384]{2,1,0:T(8,128)(2,1)}, bf16[2,96,384]{2,1,0:T(8,128)(2,1)}, bf16[2,96,384]{2,1,0:T(8,128)(2,1)}) fusion(bf16[1,2,384,384]{3,2,1,0:T(8,128)(2,1)} %param.9, s32[]{:T(128)S(6)} %select_n.159, s32[]{:T(128)S(6)} %select_n.161, s32[]{:T(128)S(6)} %select_n.163), kind=kLoop, calls=%fused_computation.119 | loop fusion | bytes 884748 | tf_op jit(solution)/shard_map/dynamic_slice | solution.py:63
  7.9 2.4 %collective-permute-start = (bf16[2,96,384]{2,1,0:T(8,128)(2,1)}, bf16[2,96,384]{2,1,0:T(8,128)(2,1)}, u32[]{:S(2)}, u32[]{:S(2)}) collective-permute-start(bf16[2,96,384]{2,1,0:T(8,128)(2,1)} %get-tuple-element.17), channel_id=1, source_target_pairs={{0,1},{1,2},{2,3},{3,0},{4,5},{5,6},{6,7},{7,4},{8,9},{9,10},{10,1... | collective-permute-start | bytes 442376 | tf_op jit(solution)/shard_map/ppermute | solution.py:64
  10.3 2.6 %collective-permute-start.1 = (bf16[2,96,384]{2,1,0:T(8,128)(2,1)}, bf16[2,96,384]{2,1,0:T(8,128)(2,1)}, u32[]{:S(2)}, u32[]{:S(2)}) collective-permute-start(bf16[2,96,384]{2,1,0:T(8,128)(2,1)} %get-tuple-element.18), channel_id=1, source_target_pairs={{0,2},{1,3},{2,0},{3,1},{4,6},{5,7},{6,4},{7,5},{8,10},{9,11},{10,... | collective-permute-start | bytes 442376 | tf_op jit(solution)/shard_map/ppermute | solution.py:64
  12.9 1.3 collective-permute-start.2
  14.7 2.6 %multiply_convert_fusion.2 = (bf16[1,384,384]{2,1,0:T(8,128)(2,1)S(1)}, bf16[1,384,384]{2,1,0:T(8,128)(2,1)S(1)}) fusion(), kind=kLoop, calls=%fused_computation.87 | loop fusion | flops 1916928 | bytes 589824 | tf_op jit(solution)/shard_map/convert.22
  17.5 0.8 convolution_bitcast_fusion.3
  35.3 0.8 convolution_bitcast_fusion.2
  45.6 1.6 %gather_fusion = bf16[6,128,128]{2,1,0:T(8,128)(2,1)S(1)} fusion(bf16[16,128,128]{2,1,0:T(8,128)(2,1)} %param.15, s32[1024]{0:T(1024)S(1)} %pad_clamp_fusion.1), kind=kCustom, calls=%fused_computation | custom fusion | bytes 393240 | tf_op jit(solution)/shard_map/gather | solution.py:133
  47.6 13.3 %all_gather.7 = f32[4,2,6,128]{3,1,2,0:T(2,128)S(1)} all-gather(f32[1,2,6,128]{3,1,2,0:T(2,128)S(1)} %bitcast_subtract_fusion), channel_id=1, replica_groups=mesh['grp'=2,'frame'=4,'coil'=4] {'coil'}, dimensions={0}, use_global_device_ids=true | all-gather | bytes 30720 | tf_op jit(solution)/shard_map/all_gather | solution.py:137
  62.2 1.6 %copy-done.1 = f32[4,2,6,128,128]{3,4,1,0,2:T(8,128)} copy-done((f32[4,2,6,128,128]{3,4,1,0,2:T(8,128)}, f32[4,2,6,128,128]{3,4,1,0,2:T(8,128)S(1)}, u32[]{:S(2)}) %copy-start.1) | copy-done | bytes 3145752
  63.9 2.5 %broadcast_in_dim.28 = f32[4,2,384,384]{2,3,1,0:T(8,128)} broadcast(f32[]{:T(128)} %constant.86.clone.1), dimensions={} | broadcast | bytes 4718596 | tf_op jit(solution)/shard_map/broadcast_in_dim | solution.py:102
  66.4 7.7 %dynamic_update_slice.18 = f32[4,2,384,384]{2,3,1,0:T(8,128)} dynamic-update-slice(f32[4,2,384,384]{2,3,1,0:T(8,128)} %broadcast_in_dim.28, f32[4,2,128,128]{2,3,1,0:T(8,128)S(1)} %slice_bitcast_fusion.11, s32[]{:T(128)} %constant.76.clone.1, s32[]{:T(128)} %constant.76.clone.1, s32[]{:T(128)S(6)} %select_n.168, s32[]{:T(128)S(6)} %select_n.169) | dynamic-update-slice | bytes 1048580 | tf_op jit(solution)/shard_map/dynamic_update_slice | solution.py:106
  74.1 1.6 %fusion.45 = f32[4,2,128,128]{2,3,1,0:T(8,128)S(1)} fusion(f32[4,2,6,128,128]{3,4,1,0,2:T(8,128)} %copy-done.1, f32[4,2,384,384]{2,3,1,0:T(8,128)} %dynamic_update_slice.18, s32[]{:T(128)S(6)} %select_n.170, s32[]{:T(128)S(6)} %select_n.171), kind=kLoop, calls=%fused_computation.102 | loop fusion | flops 131072 | bytes 1572872 | tf_op jit(solution)/shard_map/add | solution.py:106
  75.8 7.7 %dynamic_update_slice.19 = f32[4,2,384,384]{2,3,1,0:T(8,128)} dynamic-update-slice(f32[4,2,384,384]{2,3,1,0:T(8,128)} %dynamic_update_slice.18, f32[4,2,128,128]{2,3,1,0:T(8,128)S(1)} %fusion.45, s32[]{:T(128)} %constant.76.clone.1, s32[]{:T(128)} %constant.76.clone.1, s32[]{:T(128)S(6)} %select_n.170, s32[]{:T(128)S(6)} %select_n.171) | dynamic-update-slice | bytes 1048580 | tf_op jit(solution)/shard_map/dynamic_update_slice | solution.py:106
  83.5 1.6 %fusion.44 = f32[4,2,128,128]{2,3,1,0:T(8,128)S(1)} fusion(f32[4,2,6,128,128]{3,4,1,0,2:T(8,128)} %copy-done.1, f32[4,2,384,384]{2,3,1,0:T(8,128)} %dynamic_update_slice.19, s32[]{:T(128)S(6)} %select_n.172, s32[]{:T(128)S(6)} %select_n.173), kind=kLoop, calls=%fused_computation.100 | loop fusion | flops 131072 | bytes 1572872 | tf_op jit(solution)/shard_map/add | solution.py:106
  85.2 7.3 %dynamic_update_slice.20 = f32[4,2,384,384]{2,3,1,0:T(8,128)} dynamic-update-slice(f32[4,2,384,384]{2,3,1,0:T(8,128)} %dynamic_update_slice.19, f32[4,2,128,128]{2,3,1,0:T(8,128)S(1)} %fusion.44, s32[]{:T(128)} %constant.76.clone.1, s32[]{:T(128)} %constant.76.clone.1, s32[]{:T(128)S(6)} %select_n.172, s32[]{:T(128)S(6)} %select_n.173) | dynamic-update-slice | bytes 1048580 | tf_op jit(solution)/shard_map/dynamic_update_slice | solution.py:106
  92.5 1.6 %fusion.43 = f32[4,2,128,128]{2,3,1,0:T(8,128)S(1)} fusion(f32[4,2,6,128,128]{3,4,1,0,2:T(8,128)} %copy-done.1, f32[4,2,384,384]{2,3,1,0:T(8,128)} %dynamic_update_slice.20, s32[]{:T(128)S(6)} %select_n.174, s32[]{:T(128)S(6)} %select_n.175), kind=kLoop, calls=%fused_computation.98 | loop fusion | flops 131072 | bytes 1572872 | tf_op jit(solution)/shard_map/add | solution.py:106
  94.1 7.8 %dynamic_update_slice.21 = f32[4,2,384,384]{2,3,1,0:T(8,128)} dynamic-update-slice(f32[4,2,384,384]{2,3,1,0:T(8,128)} %dynamic_update_slice.20, f32[4,2,128,128]{2,3,1,0:T(8,128)S(1)} %fusion.43, s32[]{:T(128)} %constant.76.clone.1, s32[]{:T(128)} %constant.76.clone.1, s32[]{:T(128)S(6)} %select_n.174, s32[]{:T(128)S(6)} %select_n.175) | dynamic-update-slice | bytes 1048580 | tf_op jit(solution)/shard_map/dynamic_update_slice | solution.py:106
  101.9 1.6 %fusion.42 = f32[4,2,128,128]{2,3,1,0:T(8,128)S(1)} fusion(f32[4,2,6,128,128]{3,4,1,0,2:T(8,128)} %copy-done.1, f32[4,2,384,384]{2,3,1,0:T(8,128)} %dynamic_update_slice.21, s32[]{:T(128)S(6)} %select_n.176, s32[]{:T(128)S(6)} %select_n.177), kind=kLoop, calls=%fused_computation.96 | loop fusion | flops 131072 | bytes 1572872 | tf_op jit(solution)/shard_map/add | solution.py:106
  103.5 7.7 %dynamic_update_slice.22 = f32[4,2,384,384]{2,3,1,0:T(8,128)} dynamic-update-slice(f32[4,2,384,384]{2,3,1,0:T(8,128)} %dynamic_update_slice.21, f32[4,2,128,128]{2,3,1,0:T(8,128)S(1)} %fusion.42, s32[]{:T(128)} %constant.76.clone.1, s32[]{:T(128)} %constant.76.clone.1, s32[]{:T(128)S(6)} %select_n.176, s32[]{:T(128)S(6)} %select_n.177) | dynamic-update-slice | bytes 1048580 | tf_op jit(solution)/shard_map/dynamic_update_slice | solution.py:106
  111.3 1.6 %fusion.41 = f32[4,2,128,128]{2,3,1,0:T(8,128)S(1)} fusion(f32[4,2,6,128,128]{3,4,1,0,2:T(8,128)} %copy-done.1, f32[4,2,384,384]{2,3,1,0:T(8,128)} %dynamic_update_slice.22, s32[]{:T(128)S(6)} %select_n.178, s32[]{:T(128)S(6)} %select_n.179), kind=kLoop, calls=%fused_computation.94 | loop fusion | flops 131072 | bytes 1572872 | tf_op jit(solution)/shard_map/add | solution.py:106
  112.9 7.5 %dynamic_update_slice.23 = f32[4,2,384,384]{2,3,1,0:T(8,128)} dynamic-update-slice(f32[4,2,384,384]{2,3,1,0:T(8,128)} %dynamic_update_slice.22, f32[4,2,128,128]{2,3,1,0:T(8,128)S(1)} %fusion.41, s32[]{:T(128)} %constant.76.clone.1, s32[]{:T(128)} %constant.76.clone.1, s32[]{:T(128)S(6)} %select_n.178, s32[]{:T(128)S(6)} %select_n.179) | dynamic-update-slice | bytes 1048580 | tf_op jit(solution)/shard_map/dynamic_update_slice | solution.py:106
  120.5 3.3 %fusion.3 = f32[2,2,4,96,384]{4,3,0,1,2:T(8,128)S(1)} fusion(f32[4,2,384,384]{2,3,1,0:T(8,128)} %dynamic_update_slice.23, s32[]{:T(128)S(6)} %select_n.157, bf16[1,384,384]{2,1,0:T(8,128)(2,1)S(1)} %get-tuple-element.33, bf16[1,384,384]{2,1,0:T(8,128)(2,1)S(1)} %get-tuple-element.32), kind=kOutput, calls=%fused_computation.12 | convolution fusion | flops 454459392 | bytes 7667716 | tf_op jit(solution)/shard_map/aij,cbjk->abcik/dot_general | solution.py:109
  123.9 0.9 constant_dynamic-slice_fusion
  125.7 1.2 maximum_convert_fusion.1
  127.3 15.4 %all_gather.8 = bf16[2,384,384]{2,0,1:T(2,128)(2,1)S(1)} all-gather(bf16[2,96,384]{2,0,1:T(2,128)(2,1)S(1)} %copy.68), channel_id=1, replica_groups=mesh['grp'=2,'frame'=4,'coil'=4] {'coil'}, dimensions={1}, use_global_device_ids=true | all-gather | bytes 737280 | tf_op jit(solution)/shard_map/all_gather | solution.py:143
  142.7 1.0 copy.69
  143.7 1.5 %maximum_convert_fusion = f32[3,2,384,384]{2,3,1,0:T(8,128)S(1)} fusion(bf16[1,2,384,384]{2,3,1,0:T(8,128)(2,1)} %collective-permute-done.4, bf16[1,2,384,384]{2,3,1,0:T(8,128)(2,1)S(1)} %copy.49, bf16[1,2,384,384]{2,3,1,0:T(8,128)(2,1)} %collective-permute-done.3), kind=kLoop, calls=%fused_computation.11 | loop fusion | flops 2654208 | bytes 5308416 | tf_op jit(solution)/shard_map/convert_element_type | solution.py:47
  146.4 1.4 copy.73
  (64 shorter events, 8.7 us)
Async XLA Ops:
  0.0 44.9 %copy-start = (bf16[16,128,128]{2,1,0:T(8,128)(2,1)S(1)}, bf16[16,128,128]{2,1,0:T(8,128)(2,1)}, u32[]{:S(2)}) copy-start(bf16[16,128,128]{2,1,0:T(8,128)(2,1)} %param.14) | copy-start | bytes 1572868
  0.0 14.3 %copy-start.2 = (bf16[1,2,384,384]{3,2,1,0:T(8,128)(2,1)S(1)}, bf16[1,2,384,384]{3,2,1,0:T(8,128)(2,1)}, u32[]{:S(2)}) copy-start(bf16[1,2,384,384]{3,2,1,0:T(8,128)(2,1)} %param.9) | copy-start | bytes 1769476
  1.5 142.2 %collective-permute-start.3 = (bf16[1,2,384,384]{2,3,1,0:T(8,128)(2,1)S(1)}, bf16[1,2,384,384]{2,3,1,0:T(8,128)(2,1)}, u32[]{:S(2)}, u32[]{:S(2)}) collective-permute-start(bf16[1,2,384,384]{2,3,1,0:T(8,128)(2,1)S(1)} %copy.49), channel_id=1, source_target_pairs={{0,4},{4,8},{8,12},{1,5},{5,9},{9,13},{2,6},{6,10},{10,14},{3,7},{... | collective-permute-start | bytes 1769480 | tf_op jit(solution)/shard_map/ppermute | solution.py:21
  4.7 138.9 %collective-permute-start.4 = (bf16[1,2,384,384]{2,3,1,0:T(8,128)(2,1)S(1)}, bf16[1,2,384,384]{2,3,1,0:T(8,128)(2,1)}, u32[]{:S(2)}, u32[]{:S(2)}) collective-permute-start(bf16[1,2,384,384]{2,3,1,0:T(8,128)(2,1)S(1)} %copy.49), channel_id=1, source_target_pairs={{4,0},{8,4},{12,8},{5,1},{9,5},{13,9},{6,2},{10,6},{14,10},{7,3},{... | collective-permute-start | bytes 1769480 | tf_op jit(solution)/shard_map/ppermute | solution.py:23
  7.9 117.7 %collective-permute-start = (bf16[2,96,384]{2,1,0:T(8,128)(2,1)}, bf16[2,96,384]{2,1,0:T(8,128)(2,1)}, u32[]{:S(2)}, u32[]{:S(2)}) collective-permute-start(bf16[2,96,384]{2,1,0:T(8,128)(2,1)} %get-tuple-element.17), channel_id=1, source_target_pairs={{0,1},{1,2},{2,3},{3,0},{4,5},{5,6},{6,7},{7,4},{8,9},{9,10},{10,1... | collective-permute-start | bytes 442376 | tf_op jit(solution)/shard_map/ppermute | solution.py:64
  10.3 115.4 %collective-permute-start.1 = (bf16[2,96,384]{2,1,0:T(8,128)(2,1)}, bf16[2,96,384]{2,1,0:T(8,128)(2,1)}, u32[]{:S(2)}, u32[]{:S(2)}) collective-permute-start(bf16[2,96,384]{2,1,0:T(8,128)(2,1)} %get-tuple-element.18), channel_id=1, source_target_pairs={{0,2},{1,3},{2,0},{3,1},{4,6},{5,7},{6,4},{7,5},{8,10},{9,11},{10,... | collective-permute-start | bytes 442376 | tf_op jit(solution)/shard_map/ppermute | solution.py:64
  12.9 112.8 %collective-permute-start.2 = (bf16[2,96,384]{2,1,0:T(8,128)(2,1)}, bf16[2,96,384]{2,1,0:T(8,128)(2,1)}, u32[]{:S(2)}, u32[]{:S(2)}) collective-permute-start(bf16[2,96,384]{2,1,0:T(8,128)(2,1)} %get-tuple-element.19), channel_id=1, source_target_pairs={{0,3},{1,0},{2,1},{3,2},{4,7},{5,4},{6,5},{7,6},{8,11},{9,8},{10,9... | collective-permute-start | bytes 442376 | tf_op jit(solution)/shard_map/ppermute | solution.py:64
  18.3 0.7 copy-start.3
  18.3 2.6 %copy-start.4 = (s32[1,6]{1,0:T(1,128)S(1)}, s32[1,6]{1,0:T(1,128)}, u32[]{:S(2)}) copy-start(s32[1,6]{1,0:T(1,128)} %param.13) | copy-start | bytes 76
  36.1 8.8 %copy-start.6 = (s32[1,6]{1,0:T(1,128)S(1)}, s32[1,6]{1,0:T(1,128)}, u32[]{:S(2)}) copy-start(s32[1,6]{1,0:T(1,128)} %param.11) | copy-start | bytes 76
  41.4 6.2 %copy-start.5 = (f32[1,1,2,6,128]{4,2,3,1,0:T(2,128)S(1)}, f32[1,1,2,6,128]{4,2,3,1,0:T(2,128)}, u32[]{:S(2)}) copy-start(f32[1,1,2,6,128]{4,2,3,1,0:T(2,128)} %param.10) | copy-start | bytes 18436
  62.2 1.6 %copy-start.1 = (f32[4,2,6,128,128]{3,4,1,0,2:T(8,128)}, f32[4,2,6,128,128]{3,4,1,0,2:T(8,128)S(1)}, u32[]{:S(2)}) copy-start(f32[4,2,6,128,128]{3,4,1,0,2:T(8,128)S(1)} %convolution_bitcast_fusion) | copy-start | bytes 9437188

commit v2 on v1

--- a/solution.py
+++ b/solution.py
@@ -55,20 +55,34 @@
     return own_rows.astype(jnp.float32) - STEP_SIZE * (data_grad + TV_WEIGHT * tv_grad)
 
 
+def rotated(block, coil_count, shift):
+    return lax.ppermute(block, "coil", [(i, (i + shift) % coil_count) for i in range(coil_count)])
+
+
 def exchange_rows(coil_map, rows, coil_count, coil_index):
-    received = [None] * coil_count
-    received[0] = lax.dynamic_slice_in_dim(coil_map, coil_index * rows, rows, axis=1)
+    received = [lax.dynamic_slice_in_dim(coil_map, coil_index * rows, rows, axis=1)]
     for shift in range(1, coil_count):
         target = (coil_index + shift) % coil_count
         block = lax.dynamic_slice_in_dim(coil_map, target * rows, rows, axis=1)
-        received[shift] = lax.ppermute(
-            block, "coil", [(i, (i + shift) % coil_count) for i in range(coil_count)]
-        )
+        received.append(rotated(block, coil_count, shift))
     return jnp.stack(received)
 
 
-def forward_residual(transform, frame_image, coil_map, measured, row_first, col_first, row_w, col_w):
-    patch_side = col_w.shape[-1]
+def selector(first_index, extent, patch_side):
+    positions = jnp.arange(extent, dtype=jnp.int32)
+    offsets = jnp.arange(patch_side, dtype=jnp.int32)
+    wanted = first_index[:, None, None] + offsets[None, None, :]
+    return (positions[None, :, None] == wanted).astype(jnp.bfloat16)
+
+
+def pick_kernels(kernels, angle_ids):
+    choice = (angle_ids[:, None] == jnp.arange(kernels.shape[0], dtype=jnp.int32)[None, :])
+    flat = kernels.reshape(kernels.shape[0], -1)
+    picked = jnp.dot(choice.astype(kernels.dtype), flat, preferred_element_type=jnp.float32)
+    return picked.astype(kernels.dtype).reshape((angle_ids.shape[0],) + kernels.shape[1:])
+
+
+def forward_residual(transform, frame_image, coil_map, measured, row_select, col_select, row_w, col_w):
     map_planes = coil_map.astype(jnp.float32)
     image_planes = frame_image.astype(jnp.float32)
     coil_image = jnp.stack(
@@ -81,32 +95,30 @@
     half_done = combine_parts(products, 1.0).astype(jnp.bfloat16)
     products = jnp.einsum("bij,ajk->abik", half_done, transform, preferred_element_type=jnp.float32)
     kspace = combine_parts(products, 1.0).astype(jnp.bfloat16)
-    tiles = row_first.shape[0]
-    patches = jnp.stack(
-        [
-            lax.dynamic_slice(kspace, (0, row_first[g], col_first[g]), (2, patch_side, patch_side))
-            for g in range(tiles)
-        ],
-        axis=1,
-    )
+    picked_rows = jnp.einsum(
+        "gir,pik->pgrk", row_select, kspace, preferred_element_type=jnp.float32
+    ).astype(jnp.bfloat16)
+    patches = jnp.einsum(
+        "pgrk,gkq->pgrq", picked_rows, col_select, preferred_element_type=jnp.float32
+    ).astype(jnp.bfloat16)
     contracted = jnp.einsum("pgrq,gjq->pgrj", patches, col_w, preferred_element_type=jnp.float32)
     predicted = jnp.sum(contracted * row_w.astype(jnp.float32)[None], axis=2)
     return predicted - measured
 
 
-def backward_rows(transform, residuals, map_rows, row_first, col_first, row_w, col_w, coil_index):
-    coil_count, _, rows, extent = map_rows.shape
-    patch_side = col_w.shape[-1]
+def backward_rows(transform, residuals, map_rows, row_select, col_select, row_w, col_w, coil_index):
+    rows = map_rows.shape[2]
     spread = (row_w.astype(jnp.float32)[None, None] * residuals[:, :, :, None, :]).astype(jnp.bfloat16)
     spread_back = jnp.einsum("cpgrj,gjq->cpgrq", spread, col_w, preferred_element_type=jnp.float32)
-    grid = jnp.zeros((coil_count, 2, extent, extent), jnp.float32)
-    for g in range(row_first.shape[0]):
-        start = (0, 0, row_first[g], col_first[g])
-        window = lax.dynamic_slice(grid, start, (coil_count, 2, patch_side, patch_side))
-        grid = lax.dynamic_update_slice(grid, window + spread_back[:, :, g], start)
-    grid = grid.astype(jnp.bfloat16)
+    placed = jnp.einsum(
+        "cpgrq,gkq->cpgrk", spread_back.astype(jnp.bfloat16), col_select,
+        preferred_element_type=jnp.float32,
+    ).astype(jnp.bfloat16)
     row_table = lax.dynamic_slice_in_dim(transform, coil_index * rows, rows, axis=1)
-    products = jnp.einsum("aij,cbjk->abcik", row_table, grid, preferred_element_type=jnp.float32)
+    table_at = jnp.einsum(
+        "aij,gjr->aigr", row_table, row_select, preferred_element_type=jnp.float32
+    ).astype(jnp.bfloat16)
+    products = jnp.einsum("aigr,cbgrk->abcik", table_at, placed, preferred_element_type=jnp.float32)
     half_back = combine_parts(products, -1.0).astype(jnp.bfloat16)
     products = jnp.einsum("bcij,ajk->abcik", half_back, transform, preferred_element_type=jnp.float32)
     coil_back = combine_parts(products, -1.0)
@@ -121,6 +133,7 @@
 ):
     frame_count = images.shape[0]
     extent = images.shape[-1]
+    patch_side = kernel_cols.shape[-1]
     coil_count = lax.axis_size("coil")
     coil_index = lax.axis_index("coil")
     rows = extent // coil_count
@@ -129,16 +142,18 @@
     first_frame = lax.axis_index("frame") * frame_count
     frame_total = lax.axis_size("frame") * frame_count
     extended = padded(images, (("frame", 0),), 1)
-    row_w = kernel_rows[spoke_angle[0]]
-    col_w = kernel_cols[spoke_angle[0]]
+    row_w = pick_kernels(kernel_rows, spoke_angle[0])
+    col_w = pick_kernels(kernel_cols, spoke_angle[0])
+    row_select = selector(band_row[0], extent, patch_side)
+    col_select = selector(band_col[0], extent, patch_side)
     residual = forward_residual(
-        transform, images[0], coil_maps[0], kspace_data[0, 0], band_row[0], band_col[0], row_w, col_w
+        transform, images[0], coil_maps[0], kspace_data[0, 0], row_select, col_select, row_w, col_w
     )
-    residuals = lax.all_gather(residual, "coil")
-    sources = (coil_index - jnp.arange(coil_count, dtype=jnp.int32)) % coil_count
-    residuals = jnp.take(residuals, sources, axis=0)
+    residuals = jnp.stack(
+        [residual] + [rotated(residual, coil_count, shift) for shift in range(1, coil_count)]
+    )
     grad_rows = backward_rows(
-        transform, residuals, map_rows, band_row[0], band_col[0], row_w, col_w, coil_index
+        transform, residuals, map_rows, row_select, col_select, row_w, col_w, coil_index
     )
     data_grad = lax.all_gather(grad_rows.astype(jnp.bfloat16), "coil", axis=1, tiled=True)
     data_grad = data_grad.astype(jnp.float32)[None]

time: 150 us -> 65.1 us (0.43); the launches traced: 148 us -> 64.8 us
  local copies, waits for them, and re-layouts: 62.5 us -> 10.9 us
  between operations: 22.9 us -> 0.35 us
  blocking collectives: 28.7 us -> 17 us
  other arithmetic: 16.1 us -> 7.57 us
  matrix products: 6.66 us -> 12.1 us
  starting transfers between devices: 10.9 us -> 16.3 us
    dynamic_update_slice x6 -> x0, local copies, waits for them, and re-layouts: 45.8 us -> none  [backward_rows(): grid = lax.dynamic_update_slice(grid, window + spread_back[:, :, g], start)]
    all_gather x1 -> x0, blocking collectives: 13.3 us -> none  [local(): residuals = lax.all_gather(residual, 'coil')]
    add x5 -> x2, other arithmetic: 8.18 us -> 0.14 us  [selector(): wanted = first_index[:, None, None] + offsets[None, None, :]]
    ppermute x3 -> x6, starting transfers between devices: 6.33 us -> 11.1 us  [rotated(): lax.ppermute(block, 'coil', [(i, (i + shift) % coil_count) for i in range...]
    dot_general x1 -> x5, matrix products: 3.3 us -> 7.21 us  [the longest x1 3.78 us: backward_rows(): jnp.einsum('aigr,cbgrk->abcik', table_at, placed, preferred_element_type=...]
    gather x3 -> x0, local copies, waits for them, and re-layouts: 2.79 us -> none  [the longest x1 1.63 us: local(): col_w = kernel_cols[spoke_angle[0]]]
    broadcast_in_dim x1 -> x0, local copies, waits for them, and re-layouts: 2.51 us -> none  [backward_rows(): grid = jnp.zeros((coil_count, 2, extent, extent), jnp.float32)]
    unnamed x21 -> x24, local copies, waits for them, and re-layouts: 4.01 us -> 6.13 us
  transfers between devices with their start and end apart: 5 -> 8, of which waited for: 0 -> 1; matrix products, arithmetic and copies ran while one was open for 53% -> 37% of each run, Pallas kernels for 0% -> 0%
where the time goes in v2:
time: 65.1 us; the launch traced here: 64.8 us
  blocking collectives  17 us (26%)
  starting transfers between devices  16.3 us (25%)
  matrix products  12.1 us (19%)
  local copies, waits for them, and re-layouts  10.9 us (17%)
  other arithmetic  7.57 us (12%)
    all_gather x1, blocking collectives, local(): lax.all_gather(grad_rows.astype(jnp.bfloat16), 'coil', axis=1, tiled=True)  17 us
    ppermute x6, starting transfers between devices, rotated(): lax.ppermute(block, 'coil', [(i, (i + shift) % coil_count) for i in range...  11.1 us
    unnamed x24, local copies, waits for them, and re-layouts  6.13 us
    ppermute x1, starting transfers between devices, padded(): lax.ppermute(tail, axis, [(i, (i + 1) % count) for i in range(ends)])  3.87 us
    dot_general x1, matrix products, backward_rows(): jnp.einsum('aigr,cbgrk->abcik', table_at, placed, preferred_element_type=...  3.78 us
    another operation x1, other arithmetic  2.58 us
    dot_general x1, matrix products, forward_residual(): jnp.einsum('pgrq,gjq->pgrj', patches, col_w, preferred_element_type=jnp.f...  1.86 us
    convert_element_type x1, other arithmetic, apply_update(): widened = extended.astype(jnp.float32)  1.52 us
  transfers between devices with their start and end apart: 8, of which 1 were waited for; matrix products, arithmetic and copies ran while one was open for 37% of the time, Pallas kernels for 0%

profile of v2, /device:TPU:0, one launch (start us, length us, event | category | flops | bytes accessed | tf_op | source)
XLA Modules:
  0.0 64.8 jit_solution(3181471237074977384)
XLA Ops:
  0.0 1.4 %copy.24 = bf16[1,2,384,384]{2,3,1,0:T(8,128)(2,1)S(1)} copy(bf16[1,2,384,384]{3,2,1,0:T(8,128)(2,1)} %param.8) | data formatting | bytes 1179648 | tf_op args[0]
  1.4 1.3 %collective-permute-start.7 = (bf16[1,2,384,384]{2,3,1,0:T(8,128)(2,1)S(1)}, bf16[1,2,384,384]{2,3,1,0:T(8,128)(2,1)}, u32[]{:S(2)}, u32[]{:S(2)}) collective-permute-start(bf16[1,2,384,384]{2,3,1,0:T(8,128)(2,1)S(1)} %copy.24), channel_id=1, source_target_pairs={{4,0},{8,4},{12,8},{5,1},{9,5},{13,9},{6,2},{10,6},{14,10},{7,3},{... | collective-permute-start | bytes 1769480 | tf_op jit(solution)/shard_map/ppermute | solution.py:23
  2.7 3.9 %collective-permute-start.6 = (bf16[1,2,384,384]{2,3,1,0:T(8,128)(2,1)S(1)}, bf16[1,2,384,384]{2,3,1,0:T(8,128)(2,1)}, u32[]{:S(2)}, u32[]{:S(2)}) collective-permute-start(bf16[1,2,384,384]{2,3,1,0:T(8,128)(2,1)S(1)} %copy.24), channel_id=1, source_target_pairs={{0,4},{4,8},{8,12},{1,5},{5,9},{9,13},{2,6},{6,10},{10,14},{3,7},{... | collective-permute-start | bytes 1769480 | tf_op jit(solution)/shard_map/ppermute | solution.py:21
  6.6 2.6 %multiply_convert_fusion.1 = (bf16[1,384,384]{2,1,0:T(8,128)(2,1)S(1)}, bf16[1,384,384]{2,1,0:T(8,128)(2,1)S(1)}) fusion(), kind=kLoop, calls=%fused_computation.99 | loop fusion | flops 1916928 | bytes 589824 | tf_op jit(solution)/shard_map/convert.23
  9.9 0.8 %convolution_bitcast_fusion.2 = f32[2,2,384,384]{2,3,0,1:T(8,128)S(1)} fusion(bf16[1,384,384]{1,2,0:T(8,128)(2,1)S(1)} %get-tuple-element.10, bf16[1,384,384]{1,2,0:T(8,128)(2,1)S(1)} %get-tuple-element.9, bf16[1,384,384]{2,1,0:T(8,128)(2,1)S(1)} %get-tuple-element.14, bf16[1,384,384]{2,1,0:T(8,128)(2,1)S(1)} %get-tuple-element.15), kind=kOutput, calls=%fused_computation.17 | convolution fusion | flops 455344128 | bytes 3538944 | tf_op jit(solution)/shard_map/aij,bjk->abik/dot_general | solution.py:94
  10.9 0.5 copy-done.8
  11.8 1.1 %fusion.33 = bf16[1,6,128,128]{3,1,2,0:T(8,128)(2,1)} fusion(bf16[2,8,128,128]{3,2,1,0:T(8,128)(2,1)S(1)} %bitcast.236, s32[6]{0:T(128)S(1)} %bitcast.243), kind=kOutput, calls=%fused_computation.42 | convolution fusion | flops 3244128 | bytes 720920 | tf_op jit(solution)/shard_map/dot_general | solution.py:81
  12.9 0.4 fusion.14
  13.3 0.8 %copy.104 = f32[1,6,128,128]{3,2,1,0:T(8,128)} copy(f32[1,6,128,128]{3,1,2,0:T(8,128)S(1)} %fusion.14) | data formatting | bytes 786432
  14.1 0.8 %convolution_bitcast_fusion.1 = f32[2,2,384,384]{2,3,1,0:T(8,128)S(1)} fusion(bf16[1,384,384]{1,2,0:T(8,128)(2,1)S(1)} %fusion.81, bf16[1,384,384]{1,2,0:T(8,128)(2,1)S(1)} %fusion.80, bf16[1,384,384]{2,1,0:T(8,128)(2,1)S(1)} %get-tuple-element.14, bf16[1,384,384]{2,1,0:T(8,128)(2,1)S(1)} %get-tuple-element.15), kind=kOutput, calls=%fused_computation.16 | convolution fusion | flops 455344128 | bytes 3538944 | tf_op jit(solution)/shard_map/bij,ajk->abik/dot_general | solution.py:96
  15.0 0.8 %fusion.28 = bf16[2,384,6,128]{3,1,2,0:T(8,128)(2,1)S(1)} fusion(bf16[1,384,384]{1,2,0:T(8,128)(2,1)S(1)} %get-tuple-element.8, bf16[1,384,384]{1,2,0:T(8,128)(2,1)S(1)} %get-tuple-element.7, s32[6,128]{1,0:T(8,128)S(1)} %iota_add_fusion), kind=kOutput, calls=%fused_computation.40 | convolution fusion | flops 454459392 | bytes 1772544 | tf_op jit(solution)/shard_map/gir,pik->pgrk/dot_general | solution.py:98
  15.9 0.8 %copy.102 = bf16[2,384,6,128]{3,2,1,0:T(8,128)(2,1)S(1)} copy(bf16[2,384,6,128]{3,1,2,0:T(8,128)(2,1)S(1)} %fusion.28) | data formatting | bytes 2359296 | tf_op jit(solution)/shard_map/gir,pik->pgrk/dot_general | solution.py:98
  16.7 1.9 %fusion.15 = f32[2,6,128]{2,0,1:T(2,128)S(1)} fusion(bf16[2,6,128,384]{2,1,3,0:T(8,128)(2,1)S(1)} %bitcast.233, s32[6,128]{1,0:T(8,128)S(1)} %iota_add_fusion.1, f32[6,128,128]{2,1,0:T(8,128)} %bitcast.234, bf16[1,6,128,128]{3,1,2,0:T(8,128)(2,1)} %fusion.33), kind=kOutput, calls=%fused_computation.27 | convolution fusion | flops 202209792 | bytes 1778688 | tf_op jit(solution)/shard_map/pgrq,gjq->pgrj/dot_general | solution.py:104
  18.6 5.1 %collective-permute-start.5 = (f32[2,6,128]{2,0,1:T(2,128)S(1)}, f32[2,6,128]{2,0,1:T(2,128)S(1)}, u32[]{:S(2)}, u32[]{:S(2)}) collective-permute-start(f32[2,6,128]{2,0,1:T(2,128)S(1)} %bitcast_subtract_fusion), channel_id=1, source_target_pairs={{0,3},{1,0},{2,1},{3,2},{4,7},{5,4},{6,5},{7,6},{8,11},{9,8},{10,9... | collective-permute-start | bytes 18440 | tf_op jit(solution)/shard_map/ppermute | solution.py:59
  23.7 1.0 %collective-permute-start.3 = (f32[2,6,128]{2,0,1:T(2,128)S(1)}, f32[2,6,128]{2,0,1:T(2,128)S(1)}, u32[]{:S(2)}, u32[]{:S(2)}) collective-permute-start(f32[2,6,128]{2,0,1:T(2,128)S(1)} %bitcast_subtract_fusion), channel_id=1, source_target_pairs={{0,1},{1,2},{2,3},{3,0},{4,5},{5,6},{6,7},{7,4},{8,9},{9,10},{10,1... | collective-permute-start | bytes 18440 | tf_op jit(solution)/shard_map/ppermute | solution.py:59
  24.7 1.1 %fusion.30 = bf16[2,96,6,128,1,1]{3,1,2,0,5,4:T(8,128)(2,1)} fusion(s32[6,128]{1,0:T(8,128)S(1)} %iota_add_fusion, s32[]{:T(128)S(6)} %select_n.47, bf16[1,384,384]{2,1,0:T(8,128)(2,1)S(1)} %get-tuple-element.15, bf16[1,384,384]{2,1,0:T(8,128)(2,1)S(1)} %get-tuple-element.14), kind=kOutput, calls=%fused_computation.41 | convolution fusion | flops 113983488 | bytes 887812 | tf_op jit(solution)/shard_map/aij,gjr->aigr/dot_general | solution.py:118
  25.9 0.7 %constant_dynamic-slice_fusion = bf16[1,2,96,384]{3,2,0,1:T(8,128)(2,1)} fusion(bf16[1,2,384,384]{3,2,0,1:T(8,128)(2,1)S(1)} %bitcast.231, s32[]{:T(128)S(6)} %select_n.47), kind=kLoop, calls=%fused_computation.140 | loop fusion | bytes 294916 | tf_op jit(solution)/shard_map/dynamic_slice | solution.py:63
  26.5 0.8 %dynamic-slice_bitcast_fusion.2 = (bf16[2,96,384]{2,1,0:T(8,128)(2,1)}, bf16[2,96,384]{2,1,0:T(8,128)(2,1)}, bf16[2,96,384]{2,1,0:T(8,128)(2,1)}) fusion(bf16[1,2,384,384]{3,2,1,0:T(8,128)(2,1)S(1)} %copy-done, s32[]{:T(128)S(6)} %select_n.49, s32[]{:T(128)S(6)} %select_n.51, s32[]{:T(128)S(6)} %select_n.53), kind=kLoop, calls=%fused_computation.125 | loop fusion | bytes 884748 | tf_op jit(solution)/shard_map/dynamic_slice | solution.py:66
  27.3 2.5 %collective-permute-start = (bf16[2,96,384]{2,1,0:T(8,128)(2,1)}, bf16[2,96,384]{2,1,0:T(8,128)(2,1)}, u32[]{:S(2)}, u32[]{:S(2)}) collective-permute-start(bf16[2,96,384]{2,1,0:T(8,128)(2,1)} %get-tuple-element.11), channel_id=1, source_target_pairs={{0,1},{1,2},{2,3},{3,0},{4,5},{5,6},{6,7},{7,4},{8,9},{9,10},{10,1... | collective-permute-start | bytes 442376 | tf_op jit(solution)/shard_map/ppermute | solution.py:59
  29.8 0.9 %collective-permute-start.1 = (bf16[2,96,384]{2,1,0:T(8,128)(2,1)}, bf16[2,96,384]{2,1,0:T(8,128)(2,1)}, u32[]{:S(2)}, u32[]{:S(2)}) collective-permute-start(bf16[2,96,384]{2,1,0:T(8,128)(2,1)} %get-tuple-element.12), channel_id=1, source_target_pairs={{0,2},{1,3},{2,0},{3,1},{4,6},{5,7},{6,4},{7,5},{8,10},{9,11},{10,... | collective-permute-start | bytes 442376 | tf_op jit(solution)/shard_map/ppermute | solution.py:59
  30.7 1.6 %collective-permute-start.2 = (bf16[2,96,384]{2,1,0:T(8,128)(2,1)}, bf16[2,96,384]{2,1,0:T(8,128)(2,1)}, u32[]{:S(2)}, u32[]{:S(2)}) collective-permute-start(bf16[2,96,384]{2,1,0:T(8,128)(2,1)} %get-tuple-element.13), channel_id=1, source_target_pairs={{0,3},{1,0},{2,1},{3,2},{4,7},{5,4},{6,5},{7,6},{8,11},{9,8},{10,9... | collective-permute-start | bytes 442376 | tf_op jit(solution)/shard_map/ppermute | solution.py:59
  32.3 0.6 convolution_convert_fusion.2
  33.0 2.8 %copy.103 = bf16[6,128,4,2,128]{4,3,2,1,0:T(2,128)(2,1)} copy(bf16[6,128,4,2,128]{4,1,3,2,0:T(8,128)(2,1)S(1)} %convolution_convert_fusion.2) | data formatting | bytes 3145728
  35.7 3.8 %fusion.6 = f32[2,2,4,96,384]{4,3,0,1,2:T(8,128)S(1)} fusion(bf16[2,96,6,128,1,1]{3,1,2,0,5,4:T(8,128)(2,1)} %fusion.30, bf16[4,2,6,128,128]{3,1,0,4,2:T(2,128)(2,1)} %bitcast.232, s32[6,128]{1,0:T(8,128)S(1)} %iota_add_fusion.1), kind=kOutput, calls=%fused_computation.13 | convolution fusion | flops 1512603648 | bytes 4230144 | tf_op jit(solution)/shard_map/aigr,cbgrk->abcik/dot_general | solution.py:121
  39.7 0.8 %convolution_bitcast_fusion = f32[2,2,4,96,384]{4,3,2,1,0:T(8,128)S(1)} fusion(bf16[1,4,96,384]{3,2,1,0:T(8,128)(2,1)S(1)} %fusion.85, bf16[1,4,96,384]{3,2,1,0:T(8,128)(2,1)S(1)} %fusion.84, bf16[1,384,384]{2,1,0:T(8,128)(2,1)S(1)} %get-tuple-element.14, bf16[1,384,384]{2,1,0:T(8,128)(2,1)S(1)} %get-tuple-element.15), kind=kOutput, calls=%fused_computation.14 | convolution fusion | flops 455344128 | bytes 3538944 | tf_op jit(solution)/shard_map/bcij,ajk->abcik/dot_general | solution.py:123
  40.5 0.6 collective-permute-done.1
  41.1 1.2 %maximum_convert_fusion.1 = f32[4,2,96,384]{3,2,0,1:T(8,128)S(1)} fusion(bf16[1,2,96,384]{3,2,0,1:T(8,128)(2,1)} %bitcast.6, bf16[1,2,96,384]{3,2,0,1:T(8,128)(2,1)} %bitcast.4, bf16[1,2,96,384]{3,2,0,1:T(8,128)(2,1)} %bitcast.2, bf16[1,2,96,384]{3,2,0,1:T(8,128)(2,1)S(1)} %copy-done.3), kind=kLoop, calls=%fused_computation.75 | loop fusion | flops 1179648 | bytes 1769472 | tf_op jit(solution)/shard_map/convert_element_type | solution.py:125
  42.7 17.0 %all_gather.3 = bf16[2,384,384]{2,0,1:T(2,128)(2,1)S(1)} all-gather(bf16[2,96,384]{2,0,1:T(2,128)(2,1)S(1)} %copy.35), channel_id=1, replica_groups=mesh['grp'=2,'frame'=4,'coil'=4] {'coil'}, dimensions={1}, use_global_device_ids=true | all-gather | bytes 737280 | tf_op jit(solution)/shard_map/all_gather | solution.py:158
  59.7 1.0 %copy.36 = bf16[2,384,384]{1,2,0:T(8,128)(2,1)S(1)} copy(bf16[2,384,384]{2,0,1:T(2,128)(2,1)S(1)} %all_gather.3) | data formatting | bytes 1179648 | tf_op jit(solution)/shard_map/all_gather | solution.py:158
  60.7 1.5 %maximum_convert_fusion = f32[3,2,384,384]{2,3,1,0:T(8,128)S(1)} fusion(bf16[1,2,384,384]{2,3,1,0:T(8,128)(2,1)} %collective-permute-done.7, bf16[1,2,384,384]{2,3,1,0:T(8,128)(2,1)S(1)} %copy.24, bf16[1,2,384,384]{2,3,1,0:T(8,128)(2,1)} %collective-permute-done.6), kind=kLoop, calls=%fused_computation.12 | loop fusion | flops 2654208 | bytes 5308416 | tf_op jit(solution)/shard_map/convert_element_type | solution.py:47
  62.8 0.3 divide_multiply_fusion
  63.4 1.4 %copy.40 = f32[1,2,384,384]{3,2,1,0:T(8,128)} copy(f32[1,2,384,384]{2,3,1,0:T(8,128)S(1)} %fusion.19) | data formatting | bytes 2359296 | tf_op jit(solution)/shard_map/sub | solution.py:55
  (49 shorter events, 2.8 us)
Async XLA Ops:
  0.0 9.3 %copy-start = (bf16[1,2,384,384]{3,2,1,0:T(8,128)(2,1)S(1)}, bf16[1,2,384,384]{3,2,1,0:T(8,128)(2,1)}, u32[]{:S(2)}) copy-start(bf16[1,2,384,384]{3,2,1,0:T(8,128)(2,1)} %param.9) | copy-start | bytes 1769476
  1.4 59.3 %collective-permute-start.7 = (bf16[1,2,384,384]{2,3,1,0:T(8,128)(2,1)S(1)}, bf16[1,2,384,384]{2,3,1,0:T(8,128)(2,1)}, u32[]{:S(2)}, u32[]{:S(2)}) collective-permute-start(bf16[1,2,384,384]{2,3,1,0:T(8,128)(2,1)S(1)} %copy.24), channel_id=1, source_target_pairs={{4,0},{8,4},{12,8},{5,1},{9,5},{13,9},{6,2},{10,6},{14,10},{7,3},{... | collective-permute-start | bytes 1769480 | tf_op jit(solution)/shard_map/ppermute | solution.py:23
  2.7 58.0 %collective-permute-start.6 = (bf16[1,2,384,384]{2,3,1,0:T(8,128)(2,1)S(1)}, bf16[1,2,384,384]{2,3,1,0:T(8,128)(2,1)}, u32[]{:S(2)}, u32[]{:S(2)}) collective-permute-start(bf16[1,2,384,384]{2,3,1,0:T(8,128)(2,1)S(1)} %copy.24), channel_id=1, source_target_pairs={{0,4},{4,8},{8,12},{1,5},{5,9},{9,13},{2,6},{6,10},{10,14},{3,7},{... | collective-permute-start | bytes 1769480 | tf_op jit(solution)/shard_map/ppermute | solution.py:21
  10.7 0.7 %copy-start.8 = (s32[1,6]{1,0:T(1,128)S(1)}, s32[1,6]{1,0:T(1,128)}, u32[]{:S(2)}) copy-start(s32[1,6]{1,0:T(1,128)} %param.12) | copy-start | bytes 76
  10.7 0.7 %copy-start.9 = (s32[1,6]{1,0:T(1,128)S(1)}, s32[1,6]{1,0:T(1,128)}, u32[]{:S(2)}) copy-start(s32[1,6]{1,0:T(1,128)} %param.13) | copy-start | bytes 76
  10.7 1.1 %copy-start.4 = (bf16[16,128,128]{2,1,0:T(8,128)(2,1)S(1)}, bf16[16,128,128]{2,1,0:T(8,128)(2,1)}, u32[]{:S(2)}) copy-start(bf16[16,128,128]{2,1,0:T(8,128)(2,1)} %param.15) | copy-start | bytes 1572868
  10.7 1.0 %copy-start.7 = (s32[1,6]{1,0:T(1,128)S(1)}, s32[1,6]{1,0:T(1,128)}, u32[]{:S(2)}) copy-start(s32[1,6]{1,0:T(1,128)} %param.11) | copy-start | bytes 76
  10.7 2.1 %copy-start.5 = (bf16[16,128,128]{2,1,0:T(8,128)(2,1)S(1)}, bf16[16,128,128]{2,1,0:T(8,128)(2,1)}, u32[]{:S(2)}) copy-start(bf16[16,128,128]{2,1,0:T(8,128)(2,1)} %param.14) | copy-start | bytes 1572868
  16.7 1.9 %copy-start.6 = (f32[1,1,2,6,128]{4,2,3,1,0:T(2,128)S(1)}, f32[1,1,2,6,128]{4,2,3,1,0:T(2,128)}, u32[]{:S(2)}) copy-start(f32[1,1,2,6,128]{4,2,3,1,0:T(2,128)} %param.10) | copy-start | bytes 18436
  18.6 13.8 %copy-start.1 = (f32[1,6,128,128]{3,2,1,0:T(8,128)S(1)}, f32[1,6,128,128]{3,2,1,0:T(8,128)}, u32[]{:S(2)}) copy-start(f32[1,6,128,128]{3,2,1,0:T(8,128)} %copy.104) | copy-start | bytes 1179652
  18.6 13.8 %copy-start.2 = (bf16[1,6,128,128]{3,1,2,0:T(8,128)(2,1)S(1)}, bf16[1,6,128,128]{3,1,2,0:T(8,128)(2,1)}, u32[]{:S(2)}) copy-start(bf16[1,6,128,128]{3,1,2,0:T(8,128)(2,1)} %fusion.33) | copy-start | bytes 589828
  18.6 8.7 %collective-permute-start.5 = (f32[2,6,128]{2,0,1:T(2,128)S(1)}, f32[2,6,128]{2,0,1:T(2,128)S(1)}, u32[]{:S(2)}, u32[]{:S(2)}) collective-permute-start(f32[2,6,128]{2,0,1:T(2,128)S(1)} %bitcast_subtract_fusion), channel_id=1, source_target_pairs={{0,3},{1,0},{2,1},{3,2},{4,7},{5,4},{6,5},{7,6},{8,11},{9,8},{10,9... | collective-permute-start | bytes 18440 | tf_op jit(solution)/shard_map/ppermute | solution.py:59
  23.7 6.1 %collective-permute-start.4 = (f32[2,6,128]{2,0,1:T(2,128)S(1)}, f32[2,6,128]{2,0,1:T(2,128)S(1)}, u32[]{:S(2)}, u32[]{:S(2)}) collective-permute-start(f32[2,6,128]{2,0,1:T(2,128)S(1)} %bitcast_subtract_fusion), channel_id=1, source_target_pairs={{0,2},{1,3},{2,0},{3,1},{4,6},{5,7},{6,4},{7,5},{8,10},{9,11},{10,... | collective-permute-start | bytes 18440 | tf_op jit(solution)/shard_map/ppermute | solution.py:59
  23.7 7.0 %collective-permute-start.3 = (f32[2,6,128]{2,0,1:T(2,128)S(1)}, f32[2,6,128]{2,0,1:T(2,128)S(1)}, u32[]{:S(2)}, u32[]{:S(2)}) collective-permute-start(f32[2,6,128]{2,0,1:T(2,128)S(1)} %bitcast_subtract_fusion), channel_id=1, source_target_pairs={{0,1},{1,2},{2,3},{3,0},{4,5},{5,6},{6,7},{7,4},{8,9},{9,10},{10,1... | collective-permute-start | bytes 18440 | tf_op jit(solution)/shard_map/ppermute | solution.py:59
  27.3 13.2 %collective-permute-start = (bf16[2,96,384]{2,1,0:T(8,128)(2,1)}, bf16[2,96,384]{2,1,0:T(8,128)(2,1)}, u32[]{:S(2)}, u32[]{:S(2)}) collective-permute-start(bf16[2,96,384]{2,1,0:T(8,128)(2,1)} %get-tuple-element.11), channel_id=1, source_target_pairs={{0,1},{1,2},{2,3},{3,0},{4,5},{5,6},{6,7},{7,4},{8,9},{9,10},{10,1... | collective-permute-start | bytes 442376 | tf_op jit(solution)/shard_map/ppermute | solution.py:59
  29.8 11.2 %collective-permute-start.1 = (bf16[2,96,384]{2,1,0:T(8,128)(2,1)}, bf16[2,96,384]{2,1,0:T(8,128)(2,1)}, u32[]{:S(2)}, u32[]{:S(2)}) collective-permute-start(bf16[2,96,384]{2,1,0:T(8,128)(2,1)} %get-tuple-element.12), channel_id=1, source_target_pairs={{0,2},{1,3},{2,0},{3,1},{4,6},{5,7},{6,4},{7,5},{8,10},{9,11},{10,... | collective-permute-start | bytes 442376 | tf_op jit(solution)/shard_map/ppermute | solution.py:59
  30.7 10.3 %collective-permute-start.2 = (bf16[2,96,384]{2,1,0:T(8,128)(2,1)}, bf16[2,96,384]{2,1,0:T(8,128)(2,1)}, u32[]{:S(2)}, u32[]{:S(2)}) collective-permute-start(bf16[2,96,384]{2,1,0:T(8,128)(2,1)} %get-tuple-element.13), channel_id=1, source_target_pairs={{0,3},{1,0},{2,1},{3,2},{4,7},{5,4},{6,5},{7,6},{8,11},{9,8},{10,9... | collective-permute-start | bytes 442376 | tf_op jit(solution)/shard_map/ppermute | solution.py:59
  39.7 1.4 %copy-start.3 = (bf16[1,2,96,384]{3,2,0,1:T(8,128)(2,1)S(1)}, bf16[1,2,96,384]{3,2,0,1:T(8,128)(2,1)}, u32[]{:S(2)}) copy-start(bf16[1,2,96,384]{3,2,0,1:T(8,128)(2,1)} %constant_dynamic-slice_fusion) | copy-start | bytes 442372
